TPU v7x, 512 devices: a whole 4x4x16 slice. The times are simulated.
512 devices in a mesh: seq: 64 (over x, z), tp: 8 (over y, core).
Axes of the slice: x: 4, y: 4, z: 16, core: 2. Of those that a mesh axis runs over, the one named last changes fastest.
Arguments:
- hidden_in: bfloat16 [8192, 2048], P('seq', 'tp'), may hold values from -3 to 3
- norm_gain: float32 [2048], replicated, may hold values from 0.1 to 1.9
- w_query: bfloat16 [2048, 2048], P(None, 'tp'), may hold values from -0.125 to 0.125
- w_key: bfloat16 [2048, 1024], P(None, 'tp'), may hold values from -0.125 to 0.125
- w_value: bfloat16 [2048, 1024], P(None, 'tp'), may hold values from -0.125 to 0.125
- w_headgate: bfloat16 [2048, 16], P(None, 'tp'), may hold values from -0.125 to 0.125
- w_out: bfloat16 [2048, 2048], P('tp'), may hold values from -0.125 to 0.125
- q_gain: float32 [128], replicated, may hold values from 1.5 to 4
- k_gain: float32 [128], replicated, may hold values from 0.1 to 1.9
- cache_keys: bfloat16 [2, 8192, 1024], P(None, 'seq', 'tp'), as said below
- cache_values: bfloat16 [2, 8192, 1024], P(None, 'seq', 'tp'), may hold values from -6 to 6
- cached_len: int32 [8], replicated, may hold values from 0 to 8192, as said below
- group_of: int32 [8], replicated, may hold values from 0 to 1, as said below
Outputs:
- layer_out: bfloat16 [8192, 2048], P('seq', 'tp')
Inputs may be any that keep to these rules, and one draw needn't show every extreme that they name: `cache_keys`: keys of the cached positions, of order one and larger. `cached_len`: some request attends to all 8192 cached positions of its prompt, and some to none. `group_of`: every shared prompt is used by some request.
All inputs are finite; a program needn't handle non-finite values.
Results may differ from a plain program's by a relative error of at most 0.018.
Values may be sent and summed in bfloat16 or wider, within the bound.
No kernel may reach another device: no remote copies, remote signals or barrier semaphores. Data moves between devices by JAX's collectives and lax.ppermute only.
A program may use at most 64 MiB of HBM per device.

v0:
```python
import math
import jax
import jax.numpy as jnp
from jax import lax
from jax.sharding import PartitionSpec as P

SPAN = 1024
norm_eps = 1e-06
rope_base = 1000000.0
masked_score = -1e30


def shifted(value, axis, by):
    peers = lax.axis_size(axis)
    pairs = [(i, i + by) for i in range(peers) if 0 <= i + by < peers]
    return lax.ppermute(value, axis, pairs)


def head_norm(vec, gain):
    return vec * lax.rsqrt(jnp.mean(vec * vec, -1, keepdims=True) + norm_eps) * gain


def rotate(vec, positions):
    half = vec.shape[-1] // 2
    freq = jnp.exp(
        jnp.arange(half, dtype=jnp.float32) * (-2.0 * math.log(rope_base) / vec.shape[-1])
    )
    angle = positions.astype(jnp.float32)[:, None] * freq[None, :]
    shape_out = (vec.shape[0],) + (1,) * (vec.ndim - 2) + (half,)
    cosine = jnp.cos(angle).reshape(shape_out)
    sine = jnp.sin(angle).reshape(shape_out)
    first = vec[..., :half]
    second = vec[..., half:]
    return jnp.concatenate([first * cosine - second * sine, second * cosine + first * sine], -1)


def attend(state_now, queries, keys_block, values_block, visible):
    running_max, running_sum, running_acc = state_now
    scores = jnp.einsum(
        "tcgd,kcd->tcgk", queries, keys_block, preferred_element_type=jnp.float32
    ) * queries.shape[-1] ** (-0.5)
    scores = jnp.where(visible[:, None, None, :], scores, masked_score)
    new_max = jnp.maximum(running_max, jnp.max(scores, -1))
    rescale = jnp.exp(running_max - new_max)
    expo = jnp.exp(scores - new_max[..., None])
    new_sum = running_sum * rescale + jnp.sum(expo, -1)
    update = jnp.einsum(
        "tcgk,kcd->tcgd",
        expo.astype(jnp.bfloat16),
        values_block,
        preferred_element_type=jnp.float32,
    )
    return (new_max, new_sum, running_acc * rescale[..., None] + update)


def per_device(
    hidden_in,
    norm_gain,
    w_query,
    w_key,
    w_value,
    w_headgate,
    w_out,
    q_gain,
    k_gain,
    cache_keys,
    cache_values,
    cached_len,
    group_of,
):
    tok_rows = hidden_in.shape[0]
    head_dim = q_gain.shape[0]
    kv_local = w_key.shape[1] // head_dim
    heads_local = w_query.shape[1] // head_dim
    group_size = heads_local // kv_local
    per_request = SPAN // tok_rows
    seq_size = lax.axis_size("seq")
    req_count = seq_size // per_request
    gathered = lax.all_gather(hidden_in, "tp", axis=1, tiled=True)
    widened = gathered.astype(jnp.float32)
    normed = (
        widened * lax.rsqrt(jnp.mean(widened * widened, -1, keepdims=True) + norm_eps) * norm_gain
    ).astype(jnp.bfloat16)
    seq_index = lax.axis_index("seq")
    local_part = seq_index // req_count
    request = seq_index % req_count
    length = cached_len[request]
    group_id = group_of[request]
    positions = length + local_part * tok_rows + jnp.arange(tok_rows, dtype=jnp.int32)
    query_raw = jnp.dot(normed, w_query, preferred_element_type=jnp.float32).reshape(
        tok_rows, kv_local, group_size, head_dim
    )
    queries = rotate(head_norm(query_raw, q_gain), positions).astype(jnp.bfloat16)
    key_raw = jnp.dot(normed, w_key, preferred_element_type=jnp.float32).reshape(
        tok_rows, kv_local, head_dim
    )
    keys_new = rotate(head_norm(key_raw, k_gain), positions).astype(jnp.bfloat16)
    values_new = (
        jnp.dot(normed, w_value, preferred_element_type=jnp.float32)
        .astype(jnp.bfloat16)
        .reshape(tok_rows, kv_local, head_dim)
    )
    gates = jax.nn.sigmoid(jnp.dot(normed, w_headgate, preferred_element_type=jnp.float32)).reshape(
        tok_rows, kv_local, group_size
    )
    state_now = (
        jnp.full((tok_rows, kv_local, group_size), masked_score, jnp.float32),
        jnp.zeros((tok_rows, kv_local, group_size), jnp.float32),
        jnp.zeros((tok_rows, kv_local, group_size, head_dim), jnp.float32),
    )
    row_ids = jnp.arange(tok_rows, dtype=jnp.int32)
    state_now = attend(
        state_now, queries, keys_new, values_new, row_ids[None, :] <= row_ids[:, None]
    )
    all_seen = jnp.ones((1, tok_rows), bool)
    for distance in range(1, per_request):
        earlier_keys, earlier_values = shifted((keys_new, values_new), "seq", distance * req_count)
        state_now = lax.cond(
            local_part >= distance,
            lambda state_in: attend(state_in, queries, earlier_keys, earlier_values, all_seen),
            lambda state_in: state_in,
            state_now,
        )
    keys_piece = lax.all_gather(cache_keys, "seq", axis=1, tiled=True)
    values_piece = lax.all_gather(cache_values, "seq", axis=1, tiled=True)
    row_count = keys_piece.shape[1]
    keys_block = lax.dynamic_index_in_dim(keys_piece, group_id, 0, keepdims=False).reshape(
        row_count, kv_local, head_dim
    )
    values_block = lax.dynamic_index_in_dim(values_piece, group_id, 0, keepdims=False).reshape(
        row_count, kv_local, head_dim
    )
    visible = (jnp.arange(row_count, dtype=jnp.int32) < length)[None, :]
    state_now = lax.cond(
        jnp.int32(0) < length,
        lambda state_old: attend(state_old, queries, keys_block, values_block, visible),
        lambda state_old: state_old,
        state_now,
    )
    running_max, running_sum, running_acc = state_now
    mixed = (
        (running_acc / running_sum[..., None] * gates[..., None])
        .astype(jnp.bfloat16)
        .reshape(tok_rows, heads_local * head_dim)
    )
    partial_out = jnp.dot(mixed, w_out, preferred_element_type=jnp.float32)
    summed = lax.psum_scatter(
        partial_out.astype(jnp.bfloat16), "tp", scatter_dimension=1, tiled=True
    ).astype(jnp.float32)
    return (hidden_in.astype(jnp.float32) + summed).astype(jnp.bfloat16)


def solution(mesh):
    in_specs = (
        P("seq", "tp"),
        P(),
        P(None, "tp"),
        P(None, "tp"),
        P(None, "tp"),
        P(None, "tp"),
        P("tp", None),
        P(),
        P(),
        P(None, "seq", "tp"),
        P(None, "seq", "tp"),
        P(),
        P(),
    )
    out_specs = P("seq", "tp")
    return jax.shard_map(
        per_device, mesh=mesh, in_specs=in_specs, out_specs=out_specs, check_vma=False
    )
```

profile of v0, /device:TPU:2, one launch (start us, length us, event | category | flops | bytes accessed | tf_op | source)
XLA Modules:
  0.0 363.7 jit_solution(5019279901672864416)
XLA Ops:
  6.6 0.7 all-gather.3.cloned.1.call-update
  7.3 1.6 copy.86
  9.0 13.8 %all_gather.9 = bf16[128,2048]{1,0:T(8,128)(2,1)S(1)} all-gather(bf16[128,256]{1,0:T(8,128)(2,1)} %param.29), channel_id=1, replica_groups=mesh['seq'=64,'tp'=8] {'tp'}, dimensions={1}, use_global_device_ids=true | all-gather | bytes 589824 | tf_op jit(solution)/shard_map/all_gather | solution.py:79
  22.8 0.2 fusion.112
  23.0 1.4 convolution_convert_fusion.1
  24.4 17.3 %collective-permute-start.9 = (bf16[128,1,128]{2,0,1:T(8,128)(2,1)S(1)}, bf16[128,1,128]{2,0,1:T(8,128)(2,1)S(1)}, u32[]{:S(2)}, u32[]{:S(2)}) collective-permute-start(bf16[128,1,128]{2,0,1:T(8,128)(2,1)S(1)} %bitcast.382), channel_id=1, source_target_pairs={{0,320},{8,328},{16,336},{24,344},{32,352},{40,360},{48,368},{56,3... | collective-permute-start | bytes 98312 | tf_op jit(solution)/shard_map/ppermute | solution.py:16
  41.7 1.3 collective-permute-start.7
  43.0 1.3 collective-permute-start.5
  44.3 2.5 collective-permute-start.3
  46.8 2.5 collective-permute-start.1
  49.4 1.6 fusion.139
  51.1 0.2 multiply_reduce_fusion
  51.3 1.3 dynamic_slice.27
  53.4 1.5 multiply_reduce_fusion.1
  54.9 0.7 multiply_bitcast_fusion
  55.6 0.2 fusion.129
  55.9 0.3 multiply_cosine_fusion
  56.2 0.8 fusion.115
  57.0 0.3 fusion.151
  57.4 0.2 fusion.107
  57.6 0.3 fusion.111
  57.9 1.3 collective-permute-start.6
  59.2 1.8 collective-permute-start.4
  61.0 1.9 collective-permute-start.2
  63.0 11.6 %collective-permute-start = (bf16[128,1,128]{0,2,1:T(8,128)(2,1)S(1)}, bf16[128,1,128]{0,2,1:T(8,128)(2,1)S(1)}, u32[]{:S(2)}, u32[]{:S(2)}) collective-permute-start(bf16[128,1,128]{0,2,1:T(8,128)(2,1)S(1)} %pad_maximum_fusion.1), channel_id=1, source_target_pairs={{0,64},{8,72},{16,80},{24,88},{32,96},{40,104},{48,112},{56,120},{... | collective-permute-start | bytes 98312 | tf_op jit(solution)/shard_map/ppermute | solution.py:16
  74.6 0.7 collective-permute-start.13
  75.3 0.7 collective-permute-start.11
  76.0 0.7 collective-permute-start.12
  76.7 0.7 collective-permute-start.10
  77.3 1.6 collective-permute-done
  78.9 1.3 collective-permute-start.8
  81.0 0.6 conditional.8
  81.1 0.2 fusion.144
  81.3 0.2 fusion.1
  81.7 0.5 conditional.9
  81.7 0.2 fusion.145
  81.9 0.2 fusion.12
  82.3 82.6 %all-gather.3.cloned.1.call-done = bf16[2,8192,128]{2,1,0:T(8,128)(2,1)} async-done(((bf16[2,128,128]{2,1,0:T(8,128)(2,1)}), bf16[2,8192,128]{2,1,0:T(8,128)(2,1)}) %all-gather.3.cloned.1.call-update) | async-done | bytes 4194320 | tf_op jit(solution)/shard_map/all_gather | solution.py:124
  164.9 143.5 %all-gather.5.cloned.1.call-done = bf16[2,8192,128]{1,2,0:T(8,128)(2,1)} async-done(((bf16[2,128,128]{1,2,0:T(8,128)(2,1)}), bf16[2,8192,128]{1,2,0:T(8,128)(2,1)}) %all-gather.5.cloned.1.call-update) | async-done | bytes 4194320 | tf_op jit(solution)/shard_map/all_gather | solution.py:125
  308.4 11.9 %conditional.15 = (f32[128,1,2]{0,2,1:T(2,128)S(1)}, f32[128,1,2,128]{0,3,2,1:T(8,128)S(1)}) conditional(s32[]{:T(128)} %convert_element_type.107, (f32[128,1,2]{0,2,1:T(2,128)S(1)}, f32[128,1,2,128]{3,0,2,1:T(8,128)S(1)}) %tuple.71, (s32[]{:T(128)}, s32[8192]{0:T(1024)S(1)}, s32[8]{0:T(128)S(1)}, s32[]{:T(128)}, bf16[2,8192,128]{2,1,0:T(8,128)(2,1)}, ...), branch_computations={%region_33.34_spmd, %region_34.37_spmd} | conditional | flops 1088496640 | bytes 46790756 | solution.py:134
  308.4 0.6 dynamic_slice.23
  311.0 0.7 broadcast_compare_fusion
  311.8 5.8 %fusion.143 = (f32[128,2]{0,1:T(2,128)S(1)}, f32[128,1,2,8192]{0,3,2,1:T(8,128)S(1)}) fusion(bf16[128,1,2,128]{3,0,2,1:T(8,128)(2,1)S(1)} %get-tuple-element.286, bf16[2,8192,128]{2,1,0:T(8,128)(2,1)} %get-tuple-element.283, s32[]{:T(128)S(6)} %select_n.37, pred[8192]{0:T(1024)(128)(4,1)S(1)} %broadcast_compare_fusion), kind=kOutput, calls=%fused_computation.202 | convolution fusion | flops 543162112 | bytes 10560516 | tf_op jit(solution)/shard_map/cond/branch_1_fun/tcgd,kcd->tcgk/dot_general | solution.py:39
  317.6 1.6 fusion.95
  319.2 1.1 fusion.81
  320.4 1.1 convolution_convert_fusion
  321.6 34.1 %reduce-scatter.2.cloned.1.call-done = bf16[128,256]{1,0:T(8,128)(2,1)} async-done(((bf16[128,2048]{1,0:T(8,128)(2,1)}), bf16[128,256]{1,0:T(8,128)(2,1)}) %reduce-scatter.2.cloned.1.call-update) | async-done | bytes 65552 | tf_op jit(solution)/shard_map/reduce_scatter | solution.py:147
  355.6 1.5 add_convert_fusion
  (63 shorter events, 1.1 us)
Async XLA Ops:
  6.5 313.9 %copy-start = (bf16[256,2048]{1,0:T(8,128)(2,1)S(1)}, bf16[256,2048]{1,0:T(8,128)(2,1)}, u32[]{:S(2)}) copy-start(bf16[256,2048]{1,0:T(8,128)(2,1)} %param.35) | copy-start | bytes 3145732
  6.5 51.0 %copy-start.3 = (f32[2048]{0:T(1024)S(1)}, f32[2048]{0:T(1024)}, u32[]{:S(2)}) copy-start(f32[2048]{0:T(1024)} %param.30) | copy-start | bytes 24580
  6.5 51.0 %copy-start.4 = (bf16[2048,2]{0,1:T(2,128)(2,1)S(1)}, bf16[2048,2]{0,1:T(2,128)(2,1)}, u32[]{:S(2)}) copy-start(bf16[2048,2]{0,1:T(2,128)(2,1)} %param.34) | copy-start | bytes 24580
  6.5 301.9 %copy-start.5 = (s32[8]{0:T(128)S(1)}, s32[8]{0:T(128)}, u32[]{:S(2)}) copy-start(s32[8]{0:T(128)} %param.41) | copy-start | bytes 100
  6.5 158.4 %all-gather.3.cloned.1.call-start = ((), (), s32[]{:S(2)}) async-start(), calls=%async_computation.1 | async-start | bytes 4259840 | tf_op jit(solution)/shard_map/all_gather | solution.py:124
  7.3 301.1 %all-gather.5.cloned.1.call-start = ((), (), s32[]{:S(2)}) async-start(), calls=%async_computation.2 | async-start | bytes 4259840 | tf_op jit(solution)/shard_map/all_gather | solution.py:125
  8.9 346.7 %reduce-scatter.2.cloned.1.call-start = ((), (), s32[]{:S(2)}) async-start(), calls=%async_computation.3 | async-start | bytes 589824 | tf_op jit(solution)/shard_map/reduce_scatter | solution.py:147
  24.4 33.5 %collective-permute-start.9 = (bf16[128,1,128]{2,0,1:T(8,128)(2,1)S(1)}, bf16[128,1,128]{2,0,1:T(8,128)(2,1)S(1)}, u32[]{:S(2)}, u32[]{:S(2)}) collective-permute-start(bf16[128,1,128]{2,0,1:T(8,128)(2,1)S(1)} %bitcast.382), channel_id=1, source_target_pairs={{0,320},{8,328},{16,336},{24,344},{32,352},{40,360},{48,368},{56,3... | collective-permute-start | bytes 98312 | tf_op jit(solution)/shard_map/ppermute | solution.py:16
  41.7 17.5 %collective-permute-start.7 = (bf16[128,1,128]{2,0,1:T(8,128)(2,1)S(1)}, bf16[128,1,128]{2,0,1:T(8,128)(2,1)S(1)}, u32[]{:S(2)}, u32[]{:S(2)}) collective-permute-start(bf16[128,1,128]{2,0,1:T(8,128)(2,1)S(1)} %bitcast.383), channel_id=1, source_target_pairs={{0,256},{8,264},{16,272},{24,280},{32,288},{40,296},{48,304},{56,3... | collective-permute-start | bytes 98312 | tf_op jit(solution)/shard_map/ppermute | solution.py:16
  43.0 18.0 %collective-permute-start.5 = (bf16[128,1,128]{2,0,1:T(8,128)(2,1)S(1)}, bf16[128,1,128]{2,0,1:T(8,128)(2,1)S(1)}, u32[]{:S(2)}, u32[]{:S(2)}) collective-permute-start(bf16[128,1,128]{2,0,1:T(8,128)(2,1)S(1)} %bitcast.384), channel_id=1, source_target_pairs={{0,192},{8,200},{16,208},{24,216},{32,224},{40,232},{48,240},{56,2... | collective-permute-start | bytes 98312 | tf_op jit(solution)/shard_map/ppermute | solution.py:16
  44.3 18.6 %collective-permute-start.3 = (bf16[128,1,128]{2,0,1:T(8,128)(2,1)S(1)}, bf16[128,1,128]{2,0,1:T(8,128)(2,1)S(1)}, u32[]{:S(2)}, u32[]{:S(2)}) collective-permute-start(bf16[128,1,128]{2,0,1:T(8,128)(2,1)S(1)} %bitcast.385), channel_id=1, source_target_pairs={{0,128},{8,136},{16,144},{24,152},{32,160},{40,168},{48,176},{56,1... | collective-permute-start | bytes 98312 | tf_op jit(solution)/shard_map/ppermute | solution.py:16
  46.8 27.8 %collective-permute-start.1 = (bf16[128,1,128]{2,0,1:T(8,128)(2,1)S(1)}, bf16[128,1,128]{2,0,1:T(8,128)(2,1)S(1)}, u32[]{:S(2)}, u32[]{:S(2)}) collective-permute-start(bf16[128,1,128]{2,0,1:T(8,128)(2,1)S(1)} %bitcast.386), channel_id=1, source_target_pairs={{0,64},{8,72},{16,80},{24,88},{32,96},{40,104},{48,112},{56,120},{... | collective-permute-start | bytes 98312 | tf_op jit(solution)/shard_map/ppermute | solution.py:16
  57.9 17.4 %collective-permute-start.6 = (bf16[128,1,128]{0,2,1:T(8,128)(2,1)S(1)}, bf16[128,1,128]{0,2,1:T(8,128)(2,1)S(1)}, u32[]{:S(2)}, u32[]{:S(2)}) collective-permute-start(bf16[128,1,128]{0,2,1:T(8,128)(2,1)S(1)} %pad_maximum_fusion.1), channel_id=1, source_target_pairs={{0,256},{8,264},{16,272},{24,280},{32,288},{40,296},{48,304},{56,3... | collective-permute-start | bytes 98312 | tf_op jit(solution)/shard_map/ppermute | solution.py:16
  59.2 16.7 %collective-permute-start.4 = (bf16[128,1,128]{0,2,1:T(8,128)(2,1)S(1)}, bf16[128,1,128]{0,2,1:T(8,128)(2,1)S(1)}, u32[]{:S(2)}, u32[]{:S(2)}) collective-permute-start(bf16[128,1,128]{0,2,1:T(8,128)(2,1)S(1)} %pad_maximum_fusion.1), channel_id=1, source_target_pairs={{0,192},{8,200},{16,208},{24,216},{32,224},{40,232},{48,240},{56,2... | collective-permute-start | bytes 98312 | tf_op jit(solution)/shard_map/ppermute | solution.py:16
  61.0 15.6 %collective-permute-start.2 = (bf16[128,1,128]{0,2,1:T(8,128)(2,1)S(1)}, bf16[128,1,128]{0,2,1:T(8,128)(2,1)S(1)}, u32[]{:S(2)}, u32[]{:S(2)}) collective-permute-start(bf16[128,1,128]{0,2,1:T(8,128)(2,1)S(1)} %pad_maximum_fusion.1), channel_id=1, source_target_pairs={{0,128},{8,136},{16,144},{24,152},{32,160},{40,168},{48,176},{56,1... | collective-permute-start | bytes 98312 | tf_op jit(solution)/shard_map/ppermute | solution.py:16
  63.0 15.9 %collective-permute-start = (bf16[128,1,128]{0,2,1:T(8,128)(2,1)S(1)}, bf16[128,1,128]{0,2,1:T(8,128)(2,1)S(1)}, u32[]{:S(2)}, u32[]{:S(2)}) collective-permute-start(bf16[128,1,128]{0,2,1:T(8,128)(2,1)S(1)} %pad_maximum_fusion.1), channel_id=1, source_target_pairs={{0,64},{8,72},{16,80},{24,88},{32,96},{40,104},{48,112},{56,120},{... | collective-permute-start | bytes 98312 | tf_op jit(solution)/shard_map/ppermute | solution.py:16
  74.6 7.7 %collective-permute-start.13 = (bf16[128,1,128]{2,0,1:T(8,128)(2,1)S(1)}, bf16[128,1,128]{2,0,1:T(8,128)(2,1)S(1)}, u32[]{:S(2)}, u32[]{:S(2)}) collective-permute-start(bf16[128,1,128]{2,0,1:T(8,128)(2,1)S(1)} %bitcast.387), channel_id=1, source_target_pairs={{0,448},{8,456},{16,464},{24,472},{32,480},{40,488},{48,496},{56,5... | collective-permute-start | bytes 98312 | tf_op jit(solution)/shard_map/ppermute | solution.py:16
  75.3 7.0 %collective-permute-start.11 = (bf16[128,1,128]{2,0,1:T(8,128)(2,1)S(1)}, bf16[128,1,128]{2,0,1:T(8,128)(2,1)S(1)}, u32[]{:S(2)}, u32[]{:S(2)}) collective-permute-start(bf16[128,1,128]{2,0,1:T(8,128)(2,1)S(1)} %bitcast.388), channel_id=1, source_target_pairs={{0,384},{8,392},{16,400},{24,408},{32,416},{40,424},{48,432},{56,4... | collective-permute-start | bytes 98312 | tf_op jit(solution)/shard_map/ppermute | solution.py:16
  76.0 6.3 %collective-permute-start.12 = (bf16[128,1,128]{0,2,1:T(8,128)(2,1)S(1)}, bf16[128,1,128]{0,2,1:T(8,128)(2,1)S(1)}, u32[]{:S(2)}, u32[]{:S(2)}) collective-permute-start(bf16[128,1,128]{0,2,1:T(8,128)(2,1)S(1)} %pad_maximum_fusion.1), channel_id=1, source_target_pairs={{0,448},{8,456},{16,464},{24,472},{32,480},{40,488},{48,496},{56,5... | collective-permute-start | bytes 98312 | tf_op jit(solution)/shard_map/ppermute | solution.py:16
  76.7 5.6 %collective-permute-start.10 = (bf16[128,1,128]{0,2,1:T(8,128)(2,1)S(1)}, bf16[128,1,128]{0,2,1:T(8,128)(2,1)S(1)}, u32[]{:S(2)}, u32[]{:S(2)}) collective-permute-start(bf16[128,1,128]{0,2,1:T(8,128)(2,1)S(1)} %pad_maximum_fusion.1), channel_id=1, source_target_pairs={{0,384},{8,392},{16,400},{24,408},{32,416},{40,424},{48,432},{56,4... | collective-permute-start | bytes 98312 | tf_op jit(solution)/shard_map/ppermute | solution.py:16
  78.9 3.3 collective-permute-start.8
  308.4 47.2 %copy-start.2 = (bf16[128,256]{1,0:T(8,128)(2,1)S(1)}, bf16[128,256]{1,0:T(8,128)(2,1)}, u32[]{:S(2)}) copy-start(bf16[128,256]{1,0:T(8,128)(2,1)} %param.29) | copy-start | bytes 196612
  311.8 5.8 %copy-start.1 = (bf16[2,8192,128]{1,2,0:T(8,128)(2,1)S(1)}, bf16[2,8192,128]{1,2,0:T(8,128)(2,1)}, u32[]{:S(2)}) copy-start(bf16[2,8192,128]{1,2,0:T(8,128)(2,1)} %get-tuple-element.288) | copy-start | bytes 12582916 | tf_op jit(solution)/shard_map/cond
Sparse Core Ops, SparseCore 0:
  10.3 154.5 all-gather.2
  167.8 140.5 all-gather.4
  321.7 33.9 reduce-scatter.1
where the time goes:
time: 364 us
  waiting for transfers between devices  262 us (72%)
  starting transfers between devices  45.5 us (12%)
  between operations  14.9 us (4%)
  matrix products  14.7 us (4%)
  blocking collectives  13.8 us (4%)
  other arithmetic  6.18 us (2%)
  local copies, waits for them, and re-layouts  3.84 us (1%)
    all_gather x1, waiting for transfers between devices, per_device(): values_piece = lax.all_gather(cache_values, 'seq', axis=1, tiled=True)  143 us
    all_gather x1, waiting for transfers between devices, per_device(): keys_piece = lax.all_gather(cache_keys, 'seq', axis=1, tiled=True)  82.6 us
    ppermute x14, starting transfers between devices, shifted(): return lax.ppermute(value, axis, pairs)  45.4 us
    reduce_scatter x1, waiting for transfers between devices, per_device(): lax.psum_scatter(partial_out.astype(jnp.bfloat16), 'tp', scatter_dimensio...  34.1 us
    all_gather x1, blocking collectives, per_device(): gathered = lax.all_gather(hidden_in, 'tp', axis=1, tiled=True)  13.8 us
  transfers between devices with their start and end apart: 17, of which 4 were waited for; matrix products, arithmetic and copies ran while one was open for 3% of the time, Pallas kernels for 0%

commit v1 on v0

--- a/solution.py
+++ b/solution.py
@@ -122,7 +122,9 @@
             state_now,
         )
     keys_piece = lax.all_gather(cache_keys, "seq", axis=1, tiled=True)
-    values_piece = lax.all_gather(cache_values, "seq", axis=1, tiled=True)
+    values_piece = jnp.concatenate(
+        lax.all_to_all(jnp.stack([cache_values] * lax.axis_size("seq")), "seq", 0, 0), axis=1
+    )
     row_count = keys_piece.shape[1]
     keys_block = lax.dynamic_index_in_dim(keys_piece, group_id, 0, keepdims=False).reshape(
         row_count, kv_local, head_dim

time: 364 us -> 343 us (0.942)
  waiting for transfers between devices: 262 us -> 209 us
  starting transfers between devices: 45.5 us -> 74.1 us
  local copies, waits for them, and re-layouts: 3.84 us -> 10.5 us
    ppermute x14, waiting for transfers between devices: 1.63 us -> 161 us  [shifted(): return lax.ppermute(value, axis, pairs)]
    all_gather x1 -> x0, waiting for transfers between devices: 143 us -> none  [per_device(): values_piece = lax.all_gather(cache_values, 'seq', axis=1, tiled=True)]
    all_gather x1, waiting for transfers between devices: 82.6 us -> 0.02 us  [per_device(): keys_piece = lax.all_gather(cache_keys, 'seq', axis=1, tiled=True)]
    all_to_all x0 -> x1, starting transfers between devices: none -> 19 us  [per_device(): lax.all_to_all(jnp.stack([cache_values] * lax.axis_size('seq')), 'seq', 0...]
    reduce_scatter x1, waiting for transfers between devices: 34.1 us -> 46.6 us  [per_device(): lax.psum_scatter(partial_out.astype(jnp.bfloat16), 'tp', scatter_dimensio...]
    ppermute x14, starting transfers between devices: 45.4 us -> 55 us  [shifted(): return lax.ppermute(value, axis, pairs)]
    reshape x0 -> x1, local copies, waits for them, and re-layouts: none -> 4.79 us  [per_device(): jnp.concatenate(lax.all_to_all(jnp.stack([cache_values] * lax.axis_size('...]
  transfers between devices with their start and end apart: 17 -> 17, of which waited for: 4 -> 3; matrix products, arithmetic and copies ran while one was open for 3% -> 2% of each run, Pallas kernels for 0% -> 0%
where the time goes in v1:
time: 343 us
  waiting for transfers between devices  209 us (61%)
  starting transfers between devices  74.1 us (22%)
  between operations  15.3 us (4%)
  blocking collectives  13.6 us (4%)
  matrix products  13.4 us (4%)
  local copies, waits for them, and re-layouts  10.5 us (3%)
  other arithmetic  4.87 us (1%)
    ppermute x14, waiting for transfers between devices, shifted(): return lax.ppermute(value, axis, pairs)  161 us
    ppermute x14, starting transfers between devices, shifted(): return lax.ppermute(value, axis, pairs)  55 us
    reduce_scatter x1, waiting for transfers between devices, per_device(): lax.psum_scatter(partial_out.astype(jnp.bfloat16), 'tp', scatter_dimensio...  46.6 us
    all_to_all x1, starting transfers between devices, per_device(): lax.all_to_all(jnp.stack([cache_values] * lax.axis_size('seq')), 'seq', 0...  19 us
    all_gather x1, blocking collectives, per_device(): gathered = lax.all_gather(hidden_in, 'tp', axis=1, tiled=True)  13.6 us
  transfers between devices with their start and end apart: 17, of which 3 were waited for; matrix products, arithmetic and copies ran while one was open for 2% of the time, Pallas kernels for 0%

profile of v1, /device:TPU:2, one launch (start us, length us, event | category | flops | bytes accessed | tf_op | source)
XLA Modules:
  0.0 342.5 jit_solution(13644375340982271257)
XLA Ops:
  6.5 1.0 copy.87
  7.6 3.0 stack.2
  10.6 19.0 %all-to-all-start = ((bf16[64,2,128,128]{2,3,1,0:T(8,128)(2,1)}), bf16[64,2,128,128]{2,3,1,0:T(8,128)(2,1)}, u32[]{:S(2)}, u32[]{:S(2)}) async-start(bf16[64,2,128,128]{2,3,1,0:T(8,128)(2,1)} %stack.2), calls=%async_computation | async-start | bytes 8388608 | tf_op jit(solution)/shard_map/all_to_all | solution.py:126
  29.7 0.7 all-gather.2.cloned.1.call-update
  30.4 13.6 %all_gather.6 = bf16[128,2048]{1,0:T(8,128)(2,1)S(1)} all-gather(bf16[128,256]{1,0:T(8,128)(2,1)S(1)} %copy-done.2), channel_id=1, replica_groups=mesh['seq'=64,'tp'=8] {'tp'}, dimensions={1}, use_global_device_ids=true | all-gather | bytes 589824 | tf_op jit(solution)/shard_map/all_gather | solution.py:79
  44.1 0.2 fusion.112
  44.3 1.4 convolution_convert_fusion.1
  45.7 13.8 %collective-permute-start.9 = (bf16[128,1,128]{2,0,1:T(8,128)(2,1)S(1)}, bf16[128,1,128]{2,0,1:T(8,128)(2,1)S(1)}, u32[]{:S(2)}, u32[]{:S(2)}) collective-permute-start(bf16[128,1,128]{2,0,1:T(8,128)(2,1)S(1)} %bitcast.388), channel_id=1, source_target_pairs={{0,320},{8,328},{16,336},{24,344},{32,352},{40,360},{48,368},{56,3... | collective-permute-start | bytes 98312 | tf_op jit(solution)/shard_map/ppermute | solution.py:16
  59.5 1.3 collective-permute-start.7
  60.8 1.3 collective-permute-start.5
  62.1 2.5 collective-permute-start.3
  64.6 2.5 collective-permute-start.1
  67.2 0.4 fusion.139
  67.6 0.2 multiply_reduce_fusion
  67.9 0.7 dynamic_slice.27
  69.3 1.5 multiply_reduce_fusion.1
  70.9 0.2 fusion.129
  71.1 0.3 multiply_cosine_fusion
  71.7 0.3 fusion.151
  72.0 0.2 fusion.107
  72.2 0.3 fusion.111
  72.5 157.9 %collective-permute-done.9 = bf16[128,1,128]{2,0,1:T(8,128)(2,1)S(1)} collective-permute-done((bf16[128,1,128]{2,0,1:T(8,128)(2,1)S(1)}, bf16[128,1,128]{2,0,1:T(8,128)(2,1)S(1)}, u32[]{:S(2)}, u32[]{:S(2)}) %collective-permute-start.9) | collective-permute-done | bytes 32800 | tf_op jit(solution)/shard_map/ppermute | solution.py:16
  230.4 14.3 %collective-permute-start.6 = (bf16[128,1,128]{0,2,1:T(8,128)(2,1)S(1)}, bf16[128,1,128]{0,2,1:T(8,128)(2,1)S(1)}, u32[]{:S(2)}, u32[]{:S(2)}) collective-permute-start(bf16[128,1,128]{0,2,1:T(8,128)(2,1)S(1)} %pad_maximum_fusion.1), channel_id=1, source_target_pairs={{0,256},{8,264},{16,272},{24,280},{32,288},{40,296},{48,304},{56,3... | collective-permute-start | bytes 98312 | tf_op jit(solution)/shard_map/ppermute | solution.py:16
  244.8 1.3 collective-permute-start.4
  246.1 3.8 %collective-permute-start.2 = (bf16[128,1,128]{0,2,1:T(8,128)(2,1)S(1)}, bf16[128,1,128]{0,2,1:T(8,128)(2,1)S(1)}, u32[]{:S(2)}, u32[]{:S(2)}) collective-permute-start(bf16[128,1,128]{0,2,1:T(8,128)(2,1)S(1)} %pad_maximum_fusion.1), channel_id=1, source_target_pairs={{0,128},{8,136},{16,144},{24,152},{32,160},{40,168},{48,176},{56,1... | collective-permute-start | bytes 98312 | tf_op jit(solution)/shard_map/ppermute | solution.py:16
  249.9 10.2 %collective-permute-start = (bf16[128,1,128]{0,2,1:T(8,128)(2,1)S(1)}, bf16[128,1,128]{0,2,1:T(8,128)(2,1)S(1)}, u32[]{:S(2)}, u32[]{:S(2)}) collective-permute-start(bf16[128,1,128]{0,2,1:T(8,128)(2,1)S(1)} %pad_maximum_fusion.1), channel_id=1, source_target_pairs={{0,64},{8,72},{16,80},{24,88},{32,96},{40,104},{48,112},{56,120},{... | collective-permute-start | bytes 98312 | tf_op jit(solution)/shard_map/ppermute | solution.py:16
  260.2 0.7 collective-permute-start.13
  260.8 0.7 collective-permute-start.11
  261.5 0.7 collective-permute-start.12
  262.2 0.7 collective-permute-start.10
  262.9 3.3 collective-permute-done
  266.2 1.3 collective-permute-start.8
  268.3 0.6 conditional.8
  268.4 0.2 fusion.144
  268.6 0.2 fusion.1
  268.9 0.5 conditional.9
  269.0 0.2 fusion.145
  269.2 0.2 fusion.12
  269.7 16.7 %conditional.15 = (f32[128,1,2]{0,2,1:T(2,128)S(1)}, f32[128,1,2,128]{0,3,2,1:T(8,128)S(1)}) conditional(s32[]{:T(128)} %convert_element_type.107, (f32[128,1,2]{0,2,1:T(2,128)S(1)}, f32[128,1,2,128]{3,0,2,1:T(8,128)S(1)}) %tuple.71, (s32[]{:T(128)}, s32[8192]{0:T(1024)S(1)}, s32[8]{0:T(128)S(1)}, s32[]{:T(128)}, bf16[2,8192,128]{2,1,0:T(8,128)(2,1)}, ...), branch_computations={%region_33.34_spmd, %region_34.37_spmd} | conditional | flops 1088496640 | bytes 55179364 | solution.py:136
  269.7 0.6 dynamic_slice.23
  272.2 4.8 %copy_bitcast_fusion = bf16[2,8192,128]{1,2,0:T(8,128)(2,1)} fusion(bf16[2,64,128,128]{2,3,0,1:T(8,128)(2,1)} %get-tuple-element.508), kind=kLoop, calls=%fused_computation.121 | loop fusion | bytes 8388608 | tf_op jit(solution)/shard_map/reshape | solution.py:125
  277.0 0.7 broadcast_compare_fusion
  277.8 5.8 %fusion.143 = (f32[128,2]{0,1:T(2,128)S(1)}, f32[128,1,2,8192]{0,3,2,1:T(8,128)S(1)}) fusion(bf16[128,1,2,128]{3,0,2,1:T(8,128)(2,1)S(1)} %get-tuple-element.287, bf16[2,8192,128]{2,1,0:T(8,128)(2,1)} %get-tuple-element.284, s32[]{:T(128)S(6)} %select_n.37, pred[8192]{0:T(1024)(128)(4,1)S(1)} %broadcast_compare_fusion), kind=kOutput, calls=%fused_computation.203 | convolution fusion | flops 543162112 | bytes 10560516 | tf_op jit(solution)/shard_map/cond/branch_1_fun/tcgd,kcd->tcgk/dot_general | solution.py:39
  283.7 1.6 fusion.95
  285.3 1.1 fusion.81
  286.5 1.1 convolution_convert_fusion
  287.6 46.6 %reduce-scatter.2.cloned.1.call-done = bf16[128,256]{1,0:T(8,128)(2,1)} async-done(((bf16[128,2048]{1,0:T(8,128)(2,1)}), bf16[128,256]{1,0:T(8,128)(2,1)}) %reduce-scatter.2.cloned.1.call-update) | async-done | bytes 65552 | tf_op jit(solution)/shard_map/reduce_scatter | solution.py:149
  334.2 1.5 add_convert_fusion
  (72 shorter events, 1.3 us)
Async XLA Ops:
  6.5 279.9 %copy-start = (bf16[256,2048]{1,0:T(8,128)(2,1)S(1)}, bf16[256,2048]{1,0:T(8,128)(2,1)}, u32[]{:S(2)}) copy-start(bf16[256,2048]{1,0:T(8,128)(2,1)} %param.35) | copy-start | bytes 3145732
  10.6 19.8 %copy-start.2 = (bf16[128,256]{1,0:T(8,128)(2,1)S(1)}, bf16[128,256]{1,0:T(8,128)(2,1)}, u32[]{:S(2)}) copy-start(bf16[128,256]{1,0:T(8,128)(2,1)} %param.29) | copy-start | bytes 196612
  10.6 33.7 %copy-start.6 = (f32[2048]{0:T(1024)S(1)}, f32[2048]{0:T(1024)}, u32[]{:S(2)}) copy-start(f32[2048]{0:T(1024)} %param.30) | copy-start | bytes 24580
  10.6 56.6 %copy-start.5 = (bf16[2048,256]{1,0:T(8,128)(2,1)S(1)}, bf16[2048,256]{1,0:T(8,128)(2,1)}, u32[]{:S(2)}) copy-start(bf16[2048,256]{1,0:T(8,128)(2,1)} %param.31) | copy-start | bytes 3145732
  10.6 259.1 %all-to-all-start = ((bf16[64,2,128,128]{2,3,1,0:T(8,128)(2,1)}), bf16[64,2,128,128]{2,3,1,0:T(8,128)(2,1)}, u32[]{:S(2)}, u32[]{:S(2)}) async-start(bf16[64,2,128,128]{2,3,1,0:T(8,128)(2,1)} %stack.2), calls=%async_computation | async-start | bytes 8388608 | tf_op jit(solution)/shard_map/all_to_all | solution.py:126
  29.6 38.3 %copy-start.8 = (s32[8]{0:T(128)S(1)}, s32[8]{0:T(128)}, u32[]{:S(2)}) copy-start(s32[8]{0:T(128)} %param.40) | copy-start | bytes 100
  29.6 41.2 %copy-start.3 = (f32[128]{0:T(128)S(1)}, f32[128]{0:T(128)}, u32[]{:S(2)}) copy-start(f32[128]{0:T(128)} %param.37) | copy-start | bytes 1540
  29.6 41.8 %copy-start.4 = (f32[128]{0:T(128)S(1)}, f32[128]{0:T(128)}, u32[]{:S(2)}) copy-start(f32[128]{0:T(128)} %param.36) | copy-start | bytes 1540
  29.6 42.6 %copy-start.7 = (bf16[2048,2]{0,1:T(2,128)(2,1)S(1)}, bf16[2048,2]{0,1:T(2,128)(2,1)}, u32[]{:S(2)}) copy-start(bf16[2048,2]{0,1:T(2,128)(2,1)} %param.34) | copy-start | bytes 24580
  29.6 240.0 %all-gather.2.cloned.1.call-start = ((), (), s32[]{:S(2)}) async-start(), calls=%async_computation.2 | async-start | bytes 4259840 | tf_op jit(solution)/shard_map/all_gather | solution.py:124
  30.4 303.8 %reduce-scatter.2.cloned.1.call-start = ((), (), s32[]{:S(2)}) async-start(), calls=%async_computation.3 | async-start | bytes 589824 | tf_op jit(solution)/shard_map/reduce_scatter | solution.py:149
  45.7 184.8 %collective-permute-start.9 = (bf16[128,1,128]{2,0,1:T(8,128)(2,1)S(1)}, bf16[128,1,128]{2,0,1:T(8,128)(2,1)S(1)}, u32[]{:S(2)}, u32[]{:S(2)}) collective-permute-start(bf16[128,1,128]{2,0,1:T(8,128)(2,1)S(1)} %bitcast.388), channel_id=1, source_target_pairs={{0,320},{8,328},{16,336},{24,344},{32,352},{40,360},{48,368},{56,3... | collective-permute-start | bytes 98312 | tf_op jit(solution)/shard_map/ppermute | solution.py:16
  59.5 185.3 %collective-permute-start.7 = (bf16[128,1,128]{2,0,1:T(8,128)(2,1)S(1)}, bf16[128,1,128]{2,0,1:T(8,128)(2,1)S(1)}, u32[]{:S(2)}, u32[]{:S(2)}) collective-permute-start(bf16[128,1,128]{2,0,1:T(8,128)(2,1)S(1)} %bitcast.389), channel_id=1, source_target_pairs={{0,256},{8,264},{16,272},{24,280},{32,288},{40,296},{48,304},{56,3... | collective-permute-start | bytes 98312 | tf_op jit(solution)/shard_map/ppermute | solution.py:16
  60.8 185.3 %collective-permute-start.5 = (bf16[128,1,128]{2,0,1:T(8,128)(2,1)S(1)}, bf16[128,1,128]{2,0,1:T(8,128)(2,1)S(1)}, u32[]{:S(2)}, u32[]{:S(2)}) collective-permute-start(bf16[128,1,128]{2,0,1:T(8,128)(2,1)S(1)} %bitcast.390), channel_id=1, source_target_pairs={{0,192},{8,200},{16,208},{24,216},{32,224},{40,232},{48,240},{56,2... | collective-permute-start | bytes 98312 | tf_op jit(solution)/shard_map/ppermute | solution.py:16
  62.1 187.8 %collective-permute-start.3 = (bf16[128,1,128]{2,0,1:T(8,128)(2,1)S(1)}, bf16[128,1,128]{2,0,1:T(8,128)(2,1)S(1)}, u32[]{:S(2)}, u32[]{:S(2)}) collective-permute-start(bf16[128,1,128]{2,0,1:T(8,128)(2,1)S(1)} %bitcast.391), channel_id=1, source_target_pairs={{0,128},{8,136},{16,144},{24,152},{32,160},{40,168},{48,176},{56,1... | collective-permute-start | bytes 98312 | tf_op jit(solution)/shard_map/ppermute | solution.py:16
  64.6 195.5 %collective-permute-start.1 = (bf16[128,1,128]{2,0,1:T(8,128)(2,1)S(1)}, bf16[128,1,128]{2,0,1:T(8,128)(2,1)S(1)}, u32[]{:S(2)}, u32[]{:S(2)}) collective-permute-start(bf16[128,1,128]{2,0,1:T(8,128)(2,1)S(1)} %bitcast.392), channel_id=1, source_target_pairs={{0,64},{8,72},{16,80},{24,88},{32,96},{40,104},{48,112},{56,120},{... | collective-permute-start | bytes 98312 | tf_op jit(solution)/shard_map/ppermute | solution.py:16
  71.7 198.0 %copy-start.9 = (s32[8]{0:T(128)S(1)}, s32[8]{0:T(128)}, u32[]{:S(2)}) copy-start(s32[8]{0:T(128)} %param.41) | copy-start | bytes 100
  230.4 30.4 %collective-permute-start.6 = (bf16[128,1,128]{0,2,1:T(8,128)(2,1)S(1)}, bf16[128,1,128]{0,2,1:T(8,128)(2,1)S(1)}, u32[]{:S(2)}, u32[]{:S(2)}) collective-permute-start(bf16[128,1,128]{0,2,1:T(8,128)(2,1)S(1)} %pad_maximum_fusion.1), channel_id=1, source_target_pairs={{0,256},{8,264},{16,272},{24,280},{32,288},{40,296},{48,304},{56,3... | collective-permute-start | bytes 98312 | tf_op jit(solution)/shard_map/ppermute | solution.py:16
  244.8 16.7 %collective-permute-start.4 = (bf16[128,1,128]{0,2,1:T(8,128)(2,1)S(1)}, bf16[128,1,128]{0,2,1:T(8,128)(2,1)S(1)}, u32[]{:S(2)}, u32[]{:S(2)}) collective-permute-start(bf16[128,1,128]{0,2,1:T(8,128)(2,1)S(1)} %pad_maximum_fusion.1), channel_id=1, source_target_pairs={{0,192},{8,200},{16,208},{24,216},{32,224},{40,232},{48,240},{56,2... | collective-permute-start | bytes 98312 | tf_op jit(solution)/shard_map/ppermute | solution.py:16
  246.1 16.1 %collective-permute-start.2 = (bf16[128,1,128]{0,2,1:T(8,128)(2,1)S(1)}, bf16[128,1,128]{0,2,1:T(8,128)(2,1)S(1)}, u32[]{:S(2)}, u32[]{:S(2)}) collective-permute-start(bf16[128,1,128]{0,2,1:T(8,128)(2,1)S(1)} %pad_maximum_fusion.1), channel_id=1, source_target_pairs={{0,128},{8,136},{16,144},{24,152},{32,160},{40,168},{48,176},{56,1... | collective-permute-start | bytes 98312 | tf_op jit(solution)/shard_map/ppermute | solution.py:16
  249.9 16.3 %collective-permute-start = (bf16[128,1,128]{0,2,1:T(8,128)(2,1)S(1)}, bf16[128,1,128]{0,2,1:T(8,128)(2,1)S(1)}, u32[]{:S(2)}, u32[]{:S(2)}) collective-permute-start(bf16[128,1,128]{0,2,1:T(8,128)(2,1)S(1)} %pad_maximum_fusion.1), channel_id=1, source_target_pairs={{0,64},{8,72},{16,80},{24,88},{32,96},{40,104},{48,112},{56,120},{... | collective-permute-start | bytes 98312 | tf_op jit(solution)/shard_map/ppermute | solution.py:16
  260.2 9.4 %collective-permute-start.13 = (bf16[128,1,128]{2,0,1:T(8,128)(2,1)S(1)}, bf16[128,1,128]{2,0,1:T(8,128)(2,1)S(1)}, u32[]{:S(2)}, u32[]{:S(2)}) collective-permute-start(bf16[128,1,128]{2,0,1:T(8,128)(2,1)S(1)} %bitcast.393), channel_id=1, source_target_pairs={{0,448},{8,456},{16,464},{24,472},{32,480},{40,488},{48,496},{56,5... | collective-permute-start | bytes 98312 | tf_op jit(solution)/shard_map/ppermute | solution.py:16
  260.8 8.7 %collective-permute-start.11 = (bf16[128,1,128]{2,0,1:T(8,128)(2,1)S(1)}, bf16[128,1,128]{2,0,1:T(8,128)(2,1)S(1)}, u32[]{:S(2)}, u32[]{:S(2)}) collective-permute-start(bf16[128,1,128]{2,0,1:T(8,128)(2,1)S(1)} %bitcast.394), channel_id=1, source_target_pairs={{0,384},{8,392},{16,400},{24,408},{32,416},{40,424},{48,432},{56,4... | collective-permute-start | bytes 98312 | tf_op jit(solution)/shard_map/ppermute | solution.py:16
  261.5 8.1 %collective-permute-start.12 = (bf16[128,1,128]{0,2,1:T(8,128)(2,1)S(1)}, bf16[128,1,128]{0,2,1:T(8,128)(2,1)S(1)}, u32[]{:S(2)}, u32[]{:S(2)}) collective-permute-start(bf16[128,1,128]{0,2,1:T(8,128)(2,1)S(1)} %pad_maximum_fusion.1), channel_id=1, source_target_pairs={{0,448},{8,456},{16,464},{24,472},{32,480},{40,488},{48,496},{56,5... | collective-permute-start | bytes 98312 | tf_op jit(solution)/shard_map/ppermute | solution.py:16
  262.2 7.4 %collective-permute-start.10 = (bf16[128,1,128]{0,2,1:T(8,128)(2,1)S(1)}, bf16[128,1,128]{0,2,1:T(8,128)(2,1)S(1)}, u32[]{:S(2)}, u32[]{:S(2)}) collective-permute-start(bf16[128,1,128]{0,2,1:T(8,128)(2,1)S(1)} %pad_maximum_fusion.1), channel_id=1, source_target_pairs={{0,384},{8,392},{16,400},{24,408},{32,416},{40,424},{48,432},{56,4... | collective-permute-start | bytes 98312 | tf_op jit(solution)/shard_map/ppermute | solution.py:16
  266.2 3.3 collective-permute-start.8
  277.8 5.8 %copy-start.1 = (bf16[2,8192,128]{1,2,0:T(8,128)(2,1)S(1)}, bf16[2,8192,128]{1,2,0:T(8,128)(2,1)}, u32[]{:S(2)}) copy-start(bf16[2,8192,128]{1,2,0:T(8,128)(2,1)} %copy_bitcast_fusion) | copy-start | bytes 12582916 | tf_op jit(solution)/shard_map/cond
Sparse Core Ops, SparseCore 0:
  33.4 220.2 all-gather.1
  287.7 46.4 reduce-scatter.1
